TPU v7x, 32 devices: a whole 2x2x4 slice. The times are simulated.
32 devices in a mesh: rep: 8 (over z, x), tile: 4 (over y, core).
Axes of the slice: x: 2, y: 2, z: 4, core: 2. Of those that a mesh axis runs over, the one named last changes fastest.
Arguments:
- features: bfloat16 [16, 48, 72, 1536], P('rep', 'tile'), may hold values from -6 to 6
- conv_out: bfloat16 [16, 48, 72, 256], P('rep', 'tile'), may hold values from -6 to 6
- conv_weight: bfloat16 [9, 1536, 256], replicated, may hold values from -0.0546875 to 0.0546875
- norm_gain_vector: float32 [256], replicated, may hold values from 0.5 to 1.5
- norm_shift_vector: float32 [256], replicated, may hold values from -3 to 3
- class_map: float32 [3, 256], replicated, may hold values from -3 to 3
- labels: int32 [16, 48, 72], P('rep', 'tile'), may hold values from 0 to 2
- class_weight: int32 [3], replicated, may hold values from 1 to 39
Outputs:
- grad_features: bfloat16 [16, 48, 72, 1536], P('rep', 'tile')
- grad_weight: float32 [1536, 9, 256], P(('rep', 'tile'))
- grad_gain: float32 [256], replicated
- grad_shift: float32 [256], replicated
- grad_class: float32 [3, 256], replicated
- loss: float32 [], replicated
All inputs are finite; a program needn't handle non-finite values.
Results may differ from a plain program's by a relative error of at most 0.0049.
Values may be sent and summed in bfloat16 or wider, within the bound.
No kernel may reach another device: no remote copies, remote signals or barrier semaphores. Data moves between devices by JAX's collectives and lax.ppermute only.
A program may use at most 256 MiB of HBM per device.

v0:
```python
import jax
import jax.numpy as jnp
from jax import lax
from jax.sharding import PartitionSpec as P

IMG_DEV = 2
H = 48
W = 72
RATE = 12


def padded(x, sides, width):
    for axis, dim in sides:
        size, length = (lax.axis_size(axis), x.shape[dim])
        up = [(i, (i + 1) % size) for i in range(size - 1)]
        down = [(j, i) for i, j in up]
        last = lax.slice_in_dim(x, length - width, length, axis=dim)
        first = lax.slice_in_dim(x, 0, width, axis=dim)
        before = lax.ppermute(last, axis, up)
        after = lax.ppermute(first, axis, down)
        x = jnp.concatenate([before, x, after], axis=dim)
    return x


def index_bits(axes):
    bits = []
    for axis in reversed(axes):
        size = lax.axis_size(axis)
        assert size & size - 1 == 0
        bits += [(axis, b) for b in range(size.bit_length() - 1)]
    return bits


def exchange(x, axis, bit):
    size = lax.axis_size(axis)
    pairs = [(i, i ^ 1 << bit) for i in range(size)]
    return lax.ppermute(x, axis, pairs)


def butterfly_sum(x, axes):
    for axis, bit in index_bits(axes):
        x = jax.tree.map(lambda v, w: v + w, x, exchange(x, axis, bit))
    return x


def halving_scatter(x, steps, bit_axes):
    bit_axes = list(bit_axes)
    for axis, bit, combined in steps:
        ax = bit_axes.index(combined)
        mine = lax.axis_index(axis) >> bit & 1
        keep = lax.dynamic_index_in_dim(x, mine, ax, keepdims=False)
        send = lax.dynamic_index_in_dim(x, 1 - mine, ax, keepdims=False)
        x = keep + exchange(send, axis, bit)
        bit_axes.pop(ax)
    return x


def body(
    features,
    conv_out,
    conv_weight,
    norm_gain_vector,
    norm_shift_vector,
    class_map,
    labels,
    class_weight,
):
    highest = lax.Precision.HIGHEST
    images, tile_rows, columns, in_chans = features.shape
    out_chans = conv_out.shape[3]
    taps = conv_weight.shape[0]
    local_pix = images * tile_rows * columns
    per_replica_part = IMG_DEV * H * W
    all_pix = lax.axis_size("rep") * per_replica_part
    classes = class_map.shape[0]
    onehot = (labels.reshape(local_pix, 1) == jnp.arange(classes, dtype=jnp.int32)).astype(
        jnp.float32
    )
    weights_pix = jnp.sum(onehot * class_weight.astype(jnp.float32), -1)
    yvals = conv_out.astype(jnp.float32).reshape(local_pix, out_chans)
    tiles = lax.axis_size("tile")
    local_sum = jnp.sum(yvals, 0)
    local_offset = yvals - local_sum / local_pix
    local_stats = jnp.concatenate(
        [local_sum, jnp.sum(local_offset * local_offset, 0), jnp.sum(weights_pix)[None]]
    )
    slot = (jnp.arange(tiles) == lax.axis_index("tile")).astype(jnp.float32)
    tile_stats = lax.psum(slot[:, None] * local_stats[None, :], "tile")
    tile_sums = tile_stats[:, :out_chans]
    column_sum = jnp.sum(tile_sums, 0)
    tile_means = tile_sums / local_pix - column_sum / per_replica_part
    variance = (
        jnp.sum(tile_stats[:, out_chans : 2 * out_chans] + local_pix * tile_means * tile_means, 0)
        / per_replica_part
    )
    weight_total = butterfly_sum(jnp.sum(tile_stats[:, 2 * out_chans]), ("rep",))
    centre_offset = yvals - column_sum / per_replica_part
    inverse_deviation = lax.rsqrt(variance + 1e-05)
    normalized_input = centre_offset * inverse_deviation
    preactivation_values = norm_gain_vector * normalized_input + norm_shift_vector
    zvals = jnp.maximum(preactivation_values, 0.0)
    logits = jnp.dot(zvals, class_map.T, precision=highest)
    top_val = jnp.max(logits, -1, keepdims=True)
    log_total = top_val[:, 0] + jnp.log(jnp.sum(jnp.exp(logits - top_val), -1))
    cross = log_total - jnp.sum(onehot * logits, -1)
    mean_weight = weight_total / all_pix
    probs = jnp.exp(logits - log_total[:, None])
    grad_logit = weights_pix[:, None] * (probs - onehot)
    class_local_slice = jnp.dot(grad_logit.T, zvals, precision=highest)
    grad_z = jnp.dot(grad_logit, class_map, precision=highest)
    preactivation_gradient = jnp.where(preactivation_values > 0, grad_z, 0.0)
    first_gradient_sum, second_gradient_sum, class_tile, loss_tile = lax.psum(
        (
            jnp.sum(preactivation_gradient, 0),
            jnp.sum(preactivation_gradient * normalized_input, 0),
            class_local_slice,
            jnp.sum(weights_pix * cross),
        ),
        "tile",
    )
    packed = jnp.concatenate(
        [first_gradient_sum, second_gradient_sum, class_tile.reshape(-1), loss_tile[None]]
    )
    normalized_output_gradient = (
        norm_gain_vector
        * inverse_deviation
        * (
            (
                preactivation_gradient
                - first_gradient_sum / per_replica_part
                - normalized_input * second_gradient_sum / per_replica_part
            )
            / mean_weight
        )
    ).astype(jnp.bfloat16)
    normalized_output_gradient = normalized_output_gradient.reshape(
        images, tile_rows, columns, out_chans
    )
    column_pad = ((0, 0), (0, 0), (RATE, RATE), (0, 0))
    extended = jnp.pad(padded(normalized_output_gradient, (("tile", 1),), RATE), column_pad)
    own_rows = jnp.pad(normalized_output_gradient, column_pad)
    shifted_list = []
    for tap_index in range(taps):
        row_off = RATE - (tap_index // 3 - 1) * RATE
        col_off = RATE - (tap_index % 3 - 1) * RATE
        if tap_index // 3 == 1:
            piece = own_rows[:, :, col_off : col_off + columns, :]
        else:
            piece = extended[:, row_off : row_off + tile_rows, col_off : col_off + columns, :]
        shifted_list.append(piece.reshape(local_pix, out_chans))
    shifted = jnp.concatenate(shifted_list, 1)
    blocks = lax.axis_size("rep") * lax.axis_size("tile")
    nbits = blocks.bit_length() - 1
    rows = in_chans // blocks
    flat_x = features.reshape(local_pix, in_chans)
    packed, flat_x = lax.optimization_barrier((packed, flat_x))
    bits = [
        (axis, bit, combined) for combined, (axis, bit) in enumerate(index_bits(("rep", "tile")))
    ]
    rest = bits[1:]
    orders = [rest, rest[1:] + rest[:1], rest[2:3] + rest[:2] + rest[3:]]
    group_taps = [taps - 2 * (taps // 3), taps // 3, taps // 3]
    starts = [sum(group_taps[:s]) for s in range(3)]
    parts = []
    for s in range(3):
        cols = jnp.concatenate(shifted_list[starts[s] : starts[s] + group_taps[s]], 1)
        part = lax.dot_general(
            flat_x, cols, (((0,), (0,)), ((), ())), preferred_element_type=jnp.float32
        )
        parts.append(part.reshape((2,) * nbits + (rows, group_taps[s] * out_chans)))
    halves = 2
    share = in_chans // halves
    grad_chunks = [
        lax.dot_general(
            shifted.reshape(local_pix, taps, out_chans),
            conv_weight[:, h * share : (h + 1) * share, :],
            (((1, 2), (0, 2)), ((), ())),
            preferred_element_type=jnp.float32,
        ).astype(jnp.bfloat16)
        for h in range(halves)
    ]
    axis, bit, combined = bits[0]
    bit_axes = list(range(nbits - 1, -1, -1))
    ax = bit_axes.index(combined)
    mine = lax.axis_index(axis) >> bit & 1
    keeps = [lax.dynamic_index_in_dim(p, mine, ax, keepdims=False) for p in parts]
    sends = [lax.dynamic_index_in_dim(p, 1 - mine, ax, keepdims=False) for p in parts]
    received = lax.optimization_barrier([exchange(v, axis, bit) for v in sends])
    bit_axes.pop(ax)
    pieces = [keeps[s] + received[s] for s in range(3)]
    small_bits = index_bits(("rep",))
    axes_of = [list(bit_axes) for s in range(3)]
    for step in range(len(rest)):
        sends, keeps = ([], [])
        for s in range(3):
            axis, bit, combined = orders[s][step]
            ax = axes_of[s].index(combined)
            mine = lax.axis_index(axis) >> bit & 1
            keeps.append(lax.dynamic_index_in_dim(pieces[s], mine, ax, keepdims=False))
            sends.append(lax.dynamic_index_in_dim(pieces[s], 1 - mine, ax, keepdims=False))
            axes_of[s].pop(ax)
        received = []
        if step < len(small_bits):
            packed, sends = lax.optimization_barrier((packed, sends))
            received.append(exchange(packed, *small_bits[step]))
        received = [
            exchange(sends[s], orders[s][step][0], orders[s][step][1]) for s in range(3)
        ] + received
        if step < halves:
            received, grad_chunks[step] = lax.optimization_barrier((received, grad_chunks[step]))
        else:
            received = lax.optimization_barrier(received)
        if step < len(small_bits):
            packed = packed + received.pop()
        pieces = [keeps[s] + received[s] for s in range(3)]
    grad_weight = jnp.concatenate(pieces, 1).reshape(rows, taps, out_chans)
    for step in range(len(rest), len(small_bits)):
        packed = packed + exchange(packed, *small_bits[step])
    grad_shift = packed[:out_chans] / mean_weight
    grad_gain = packed[out_chans : 2 * out_chans] / mean_weight
    grad_class = (
        packed[2 * out_chans : (2 + classes) * out_chans].reshape(classes, out_chans) / mean_weight
    )
    loss = packed[(2 + classes) * out_chans] / mean_weight / all_pix
    grad_features = jnp.concatenate(grad_chunks, 1).reshape(images, tile_rows, columns, in_chans)
    return (grad_features, grad_weight, grad_gain, grad_shift, grad_class, loss)


def solution(mesh):
    in_specs = (
        P("rep", "tile", None, None),
        P("rep", "tile", None, None),
        P(),
        P(),
        P(),
        P(),
        P("rep", "tile", None),
        P(),
    )
    out_specs = (P("rep", "tile", None, None), P(("rep", "tile"), None, None), P(), P(), P(), P())
    return jax.shard_map(body, mesh=mesh, in_specs=in_specs, out_specs=out_specs, check_vma=False)
```

profile of v0, /device:TPU:10, one launch (start us, length us, event | category | flops | bytes accessed | tf_op | source)
XLA Modules:
  0.0 159.8 jit_solution(8133751318955836424)
XLA Ops:
  0.7 0.8 copy.41
  1.6 0.7 convert_element_type.31
  2.2 1.4 convert_reduce_fusion
  3.6 1.5 multiply_reduce_fusion.1
  5.1 0.7 select_reduce_fusion.1
  5.8 0.7 pad_maximum_fusion.3
  6.5 11.2 %psum.35 = f32[4,513]{1,0:T(4,128)S(1)} all-reduce(f32[4,513]{1,0:T(4,128)S(1)} %broadcast_multiply_fusion), channel_id=1, replica_groups=mesh['rep'=8,'tile'=4] {'tile'}, use_global_device_ids=true, to_apply=%region_3.0 | all-reduce | flops 2052 | bytes 16416 | tf_op jit(solution)/shard_map/psum | solution.py:88
  17.7 0.6 slice_reduce_fusion.1
  18.3 0.5 collective-permute-start
  18.9 0.7 fusion.44
  19.8 1.8 %fusion.47 = (f32[1728]{0:T(1024)S(1)}, f32[1728,3]{0,1:T(4,128)S(1)}) fusion(f32[3,256]{1,0:T(4,128)S(1)} %copy-done, f32[1728,256]{1,0:T(8,128)S(1)} %fusion.26, f32[256]{0:T(256)S(1)} %copy-done.4, f32[256]{0:T(256)S(1)} %copy-done.3), kind=kOutput, calls=%fused_computation.130 | convolution fusion | flops 17255808 | bytes 1802240 | tf_op jit(solution)/shard_map/dot_general | solution.py:102
  21.6 0.6 multiply_reduce_fusion.2
  22.2 2.2 %fusion.45 = (f32[256]{0:T(256)S(1)}, f32[256]{0:T(256)S(1)}, f32[1728,256]{1,0:T(8,128)S(1)}) fusion(f32[256]{0:T(256)S(1)} %get-tuple-element.125, f32[256]{0:T(256)S(1)} %broadcast_multiply_fusion.2, bf16[2,12,72,256]{3,2,1,0:T(8,128)(2,1)S(1)} %copy-done.2, f32[3,256]{1,0:T(4,128)S(1)} %copy-done, f32[1728,3]{0,1:T(4,128)S(1)} %get-tuple-element.127, ...), kind=kOutput, calls=%fused_computation.128 | convolution fusion | flops 20374336 | bytes 4474368 | tf_op jit(solution)/shard_map/dot_general | solution.py:110
  24.4 1.0 fusion.27
  25.4 6.6 %all-reduce.2 = (f32[1]{0:T(128)}, f32[768]{0:T(1024)S(1)}, f32[256]{0:T(256)S(1)}, f32[256]{0:T(256)S(1)}) all-reduce(f32[1]{0:T(128)} %bitcast.2, f32[768]{0:T(1024)S(1)} %reshape.126, f32[256]{0:T(256)S(1)} %get-tuple-element.99, f32[256]{0:T(256)S(1)} %get-tuple-element.98), channel_id=1, replica_groups=mesh['rep'=8,'tile'=4] {'tile'}, use_global_device_ids=true, to_apply=%region_16.17 | all-reduce | flops 1281 | bytes 10248 | tf_op jit(solution)/shard_map/psum | solution.py:112
  32.0 0.7 pad_maximum_fusion.2
  33.9 1.8 %collective-permute-start.1 = (f32[]{:T(128)}, f32[]{:T(128)}, u32[]{:S(2)}, u32[]{:S(2)}) collective-permute-start(f32[]{:T(128)} %add.175), channel_id=1, source_target_pairs={{0,8},{4,12},{8,0},{12,4},{16,24},{20,28},{24,16},{28,20},{1,9},{5... | collective-permute-start | bytes 20 | tf_op jit(solution)/shard_map/ppermute | solution.py:37
  35.7 1.9 %collective-permute-done.1 = f32[]{:T(128)} collective-permute-done((f32[]{:T(128)}, f32[]{:T(128)}, u32[]{:S(2)}, u32[]{:S(2)}) %collective-permute-start.1) | collective-permute-done | bytes 36 | tf_op jit(solution)/shard_map/ppermute | solution.py:37
  38.3 4.0 %collective-permute-start.2 = (f32[]{:T(128)}, f32[]{:T(128)}, u32[]{:S(2)}, u32[]{:S(2)}) collective-permute-start(f32[]{:T(128)} %add.176), channel_id=1, source_target_pairs={{0,16},{4,20},{8,24},{12,28},{16,0},{20,4},{24,8},{28,12},{1,17},{... | collective-permute-start | bytes 20 | tf_op jit(solution)/shard_map/ppermute | solution.py:37
  42.2 0.7 collective-permute-done.2
  43.5 0.6 multiply_convert_fusion
  44.1 1.3 collective-permute-start.3
  45.5 1.3 collective-permute-start.4
  46.8 0.8 pad_slice_fusion.1
  47.6 6.7 %fusion.14 = f32[1536,768]{1,0:T(8,128)S(1)} fusion(bf16[1728,1536]{1,0:T(8,128)(2,1)} %bitcast.142, bf16[1728,256]{1,0:T(8,128)(2,1)S(1)} %bitcast.133, bf16[1728,256]{1,0:T(8,128)(2,1)S(1)} %multiply_convert_fusion, bf16[1728,256]{1,0:T(8,128)(2,1)S(1)} %bitcast.135), kind=kOutput, calls=%fused_computation.20 | convolution fusion | flops 4084826112 | bytes 12681216 | tf_op jit(solution)/shard_map/dot_general | solution.py:167
  54.3 0.4 constant_dynamic-slice_fusion.1
  55.0 1.7 %collective-permute-start.6 = (f32[2,2,2,2,48,768]{5,4,3,1,0,2:T(8,128)S(1)}, f32[2,2,2,2,48,768]{5,4,3,1,0,2:T(8,128)S(1)}, u32[]{:S(2)}, u32[]{:S(2)}) collective-permute-start(f32[2,2,2,2,48,768]{5,4,3,1,0,2:T(8,128)S(1)} %bitcast.137), channel_id=1, source_target_pairs={{0,1},{1,0},{2,3},{3,2},{4,5},{5,4},{6,7},{7,6},{8,9},{9,8},{10,11... | collective-permute-start | bytes 7077896 | tf_op jit(solution)/shard_map/ppermute | solution.py:37
  56.6 1.9 %fusion.5 = bf16[2,36,96,256]{3,2,1,0:T(8,128)(2,1)S(1)} fusion(bf16[2,12,72,256]{3,2,1,0:T(8,128)(2,1)S(1)} %collective-permute-done.4, bf16[2,12,72,256]{3,2,1,0:T(8,128)(2,1)S(1)} %bitcast.116, bf16[2,12,72,256]{3,2,1,0:T(8,128)(2,1)S(1)} %collective-permute-done.3), kind=kLoop, calls=%fused_computation.10 | loop fusion | flops 21233664 | bytes 6193152 | tf_op jit(solution)/shard_map/concatenate | solution.py:21
  58.5 0.3 fusion.46
  58.9 4.5 %fusion.20 = f32[1536,768]{1,0:T(8,128)S(1)} fusion(bf16[1728,1536]{1,0:T(8,128)(2,1)S(1)} %bitcast.146, bf16[1728,256]{1,0:T(8,128)(2,1)S(1)} %bitcast.125, bf16[1728,256]{1,0:T(8,128)(2,1)S(1)} %bitcast.121, bf16[1728,256]{1,0:T(8,128)(2,1)S(1)} %bitcast.127), kind=kOutput, calls=%fused_computation.26 | convolution fusion | flops 4084826112 | bytes 12681216 | tf_op jit(solution)/shard_map/dot_general | solution.py:167
  63.4 0.4 constant_dynamic-slice_fusion
  64.0 4.2 %collective-permute-start.7 = (f32[2,2,2,2,48,768]{5,4,3,2,0,1:T(8,128)S(1)}, f32[2,2,2,2,48,768]{5,4,3,2,0,1:T(8,128)S(1)}, u32[]{:S(2)}, u32[]{:S(2)}) collective-permute-start(f32[2,2,2,2,48,768]{5,4,3,2,0,1:T(8,128)S(1)} %bitcast.138), channel_id=1, source_target_pairs={{0,1},{1,0},{2,3},{3,2},{4,5},{5,4},{6,7},{7,6},{8,9},{9,8},{10,11... | collective-permute-start | bytes 7077896 | tf_op jit(solution)/shard_map/ppermute | solution.py:37
  68.3 6.7 %fusion.8 = f32[1536,768]{1,0:T(8,128)S(1)} fusion(bf16[1728,1536]{1,0:T(8,128)(2,1)} %bitcast.143, bf16[1728,256]{1,0:T(8,128)(2,1)S(1)} %bitcast.129, bf16[1728,256]{1,0:T(8,128)(2,1)S(1)} %bitcast.123, bf16[1728,256]{1,0:T(8,128)(2,1)S(1)} %bitcast.131), kind=kOutput, calls=%fused_computation.14 | convolution fusion | flops 4084826112 | bytes 12681216 | tf_op jit(solution)/shard_map/dot_general | solution.py:167
  75.0 0.4 constant_dynamic-slice_fusion.5
  76.3 3.9 %collective-permute-done.5 = f32[2,2,2,2,48,768]{5,4,2,1,0,3:T(8,128)S(1)} collective-permute-done((f32[2,2,2,2,48,768]{5,4,2,1,0,3:T(8,128)S(1)}, f32[2,2,2,2,48,768]{5,4,2,1,0,3:T(8,128)S(1)}, u32[]{:S(2)}, u32[]{:S(2)}) %collective-permute-start.5) | collective-permute-done | bytes 2359328 | tf_op jit(solution)/shard_map/ppermute | solution.py:37
  81.0 0.5 bitcast_add_fusion.2
  81.6 0.5 collective-permute-start.10
  82.1 1.5 collective-permute-start.9
  83.6 0.5 collective-permute-start.11
  84.1 8.6 %bitcast_convert_fusion.1 = bf16[1728,768]{1,0:T(8,128)(2,1)S(1)} fusion(bf16[1728,9,256]{2,0,1:T(8,128)(2,1)S(1)} %constant_dynamic-update-slice_fusion, bf16[9,1536,256]{2,1,0:T(8,128)(2,1)} %param.10), kind=kOutput, calls=%fused_computation.5 | convolution fusion | flops 6116622336 | bytes 14155776 | tf_op jit(solution)/shard_map/dot_general | solution.py:174
  92.7 17.3 %collective-permute-done.11 = f32[1281]{0:T(1024)S(1)} collective-permute-done((f32[1281]{0:T(1024)S(1)}, f32[1281]{0:T(1024)S(1)}, u32[]{:S(2)}, u32[]{:S(2)}) %collective-permute-start.11) | collective-permute-done | bytes 5156 | tf_op jit(solution)/shard_map/ppermute | solution.py:37
  110.0 0.3 bitcast_add_fusion.3
  110.7 1.6 collective-permute-start.12
  112.3 1.6 collective-permute-start.13
  113.8 1.7 %collective-permute-start.14 = (f32[2,2,48,768]{3,2,1,0:T(8,128)S(1)}, f32[2,2,48,768]{3,2,1,0:T(8,128)S(1)}, u32[]{:S(2)}, u32[]{:S(2)}) collective-permute-start(f32[2,2,48,768]{3,2,1,0:T(8,128)S(1)} %dynamic-slice_bitcast_fusion.3), channel_id=1, source_target_pairs={{0,2},{1,3},{2,0},{3,1},{4,6},{5,7},{6,4},{7,5},{8,10},{9,11},{10,... | collective-permute-start | bytes 1769480 | tf_op jit(solution)/shard_map/ppermute | solution.py:37
  115.6 0.5 collective-permute-start.15
  116.0 8.6 %bitcast_convert_fusion = bf16[1728,768]{1,0:T(8,128)(2,1)S(1)} fusion(bf16[1728,9,256]{2,0,1:T(8,128)(2,1)S(1)} %constant_dynamic-update-slice_fusion, bf16[9,1536,256]{2,1,0:T(8,128)(2,1)} %param.10), kind=kOutput, calls=%fused_computation.4 | convolution fusion | flops 6116622336 | bytes 14155776 | tf_op jit(solution)/shard_map/dot_general | solution.py:174
  124.6 1.8 %collective-permute-done.15 = f32[1281]{0:T(1024)S(1)} collective-permute-done((f32[1281]{0:T(1024)S(1)}, f32[1281]{0:T(1024)S(1)}, u32[]{:S(2)}, u32[]{:S(2)}) %collective-permute-start.15) | collective-permute-done | bytes 5156 | tf_op jit(solution)/shard_map/ppermute | solution.py:37
  126.4 1.1 collective-permute-done.14
  127.9 0.5 collective-permute-start.16
  128.4 2.6 %collective-permute-start.17 = (f32[2,48,768]{2,1,0:T(8,128)S(1)}, f32[2,48,768]{2,1,0:T(8,128)S(1)}, u32[]{:S(2)}, u32[]{:S(2)}) collective-permute-start(f32[2,48,768]{2,1,0:T(8,128)S(1)} %dynamic-slice_bitcast_fusion.7), channel_id=1, source_target_pairs={{0,16},{4,20},{8,24},{12,28},{16,0},{20,4},{24,8},{28,12},{1,17},{... | collective-permute-start | bytes 884744 | tf_op jit(solution)/shard_map/ppermute | solution.py:37
  131.0 0.5 collective-permute-start.18
  131.5 0.3 collective-permute-start.19
  131.9 2.8 %pad_maximum_fusion = bf16[1728,1536]{1,0:T(8,128)(2,1)} fusion(bf16[1728,768]{1,0:T(8,128)(2,1)S(1)} %bitcast_convert_fusion, bf16[1728,768]{1,0:T(8,128)(2,1)S(1)} %bitcast_convert_fusion.1), kind=kLoop, calls=%fused_computation.3 | loop fusion | flops 10616832 | bytes 10616832 | tf_op jit(solution)/shard_map/concatenate | solution.py:225
  134.7 7.6 %collective-permute-done.19 = f32[1281]{0:T(1024)S(1)} collective-permute-done((f32[1281]{0:T(1024)S(1)}, f32[1281]{0:T(1024)S(1)}, u32[]{:S(2)}, u32[]{:S(2)}) %collective-permute-start.19) | collective-permute-done | bytes 5156 | tf_op jit(solution)/shard_map/ppermute | solution.py:37
  142.3 0.5 slice.75
  143.5 0.6 div.75
  144.1 6.2 %collective-permute-start.22 = (f32[48,768]{1,0:T(8,128)S(1)}, f32[48,768]{1,0:T(8,128)S(1)}, u32[]{:S(2)}, u32[]{:S(2)}) collective-permute-start(f32[48,768]{1,0:T(8,128)S(1)} %dynamic-slice_bitcast_fusion.9), channel_id=1, source_target_pairs={{0,16},{4,20},{8,24},{12,28},{16,0},{20,4},{24,8},{28,12},{1,17},{... | collective-permute-start | bytes 442376 | tf_op jit(solution)/shard_map/ppermute | solution.py:37
  150.4 1.2 collective-permute-start.21
  151.8 0.6 slice_divide_fusion.1
  152.3 1.5 collective-permute-done.22
  153.9 1.7 %collective-permute-done.21 = f32[48,768]{1,0:T(8,128)S(1)} collective-permute-done((f32[48,768]{1,0:T(8,128)S(1)}, f32[48,768]{1,0:T(8,128)S(1)}, u32[]{:S(2)}, u32[]{:S(2)}) %collective-permute-start.21) | collective-permute-done | bytes 147488 | tf_op jit(solution)/shard_map/ppermute | solution.py:37
  155.6 2.2 %collective-permute-done.20 = f32[48,768]{1,0:T(8,128)S(1)} collective-permute-done((f32[48,768]{1,0:T(8,128)S(1)}, f32[48,768]{1,0:T(8,128)S(1)}, u32[]{:S(2)}, u32[]{:S(2)}) %collective-permute-start.20) | collective-permute-done | bytes 147488 | tf_op jit(solution)/shard_map/ppermute | solution.py:37
  157.9 0.8 copy.62
  (83 shorter events, 3.5 us)
Async XLA Ops:
  0.6 19.1 %copy-start = (f32[3,256]{1,0:T(4,128)S(1)}, f32[3,256]{1,0:T(4,128)}, u32[]{:S(2)}) copy-start(f32[3,256]{1,0:T(4,128)} %param.13) | copy-start | bytes 9220
  0.6 18.9 %copy-start.2 = (bf16[2,12,72,256]{3,2,1,0:T(8,128)(2,1)S(1)}, bf16[2,12,72,256]{3,2,1,0:T(8,128)(2,1)}, u32[]{:S(2)}) copy-start(bf16[2,12,72,256]{3,2,1,0:T(8,128)(2,1)} %param.9) | copy-start | bytes 2654212
  0.7 19.1 %copy-start.3 = (f32[256]{0:T(256)S(1)}, f32[256]{0:T(256)}, u32[]{:S(2)}) copy-start(f32[256]{0:T(256)} %param.11) | copy-start | bytes 3076
  0.7 19.1 %copy-start.4 = (f32[256]{0:T(256)S(1)}, f32[256]{0:T(256)}, u32[]{:S(2)}) copy-start(f32[256]{0:T(256)} %param.12) | copy-start | bytes 3076
  18.3 14.3 %collective-permute-start = (f32[]{:T(128)}, f32[]{:T(128)}, u32[]{:S(2)}, u32[]{:S(2)}) collective-permute-start(f32[]{:T(128)} %slice_reduce_fusion.1), channel_id=1, source_target_pairs={{0,4},{4,0},{8,12},{12,8},{16,20},{20,16},{24,28},{28,24},{1,5},{5... | collective-permute-start | bytes 20 | tf_op jit(solution)/shard_map/ppermute | solution.py:37
  33.9 3.7 %collective-permute-start.1 = (f32[]{:T(128)}, f32[]{:T(128)}, u32[]{:S(2)}, u32[]{:S(2)}) collective-permute-start(f32[]{:T(128)} %add.175), channel_id=1, source_target_pairs={{0,8},{4,12},{8,0},{12,4},{16,24},{20,28},{24,16},{28,20},{1,9},{5... | collective-permute-start | bytes 20 | tf_op jit(solution)/shard_map/ppermute | solution.py:37
  38.3 4.6 %collective-permute-start.2 = (f32[]{:T(128)}, f32[]{:T(128)}, u32[]{:S(2)}, u32[]{:S(2)}) collective-permute-start(f32[]{:T(128)} %add.176), channel_id=1, source_target_pairs={{0,16},{4,20},{8,24},{12,28},{16,0},{20,4},{24,8},{28,12},{1,17},{... | collective-permute-start | bytes 20 | tf_op jit(solution)/shard_map/ppermute | solution.py:37
  44.1 12.5 %collective-permute-start.3 = (bf16[2,12,72,256]{3,2,1,0:T(8,128)(2,1)S(1)}, bf16[2,12,72,256]{3,2,1,0:T(8,128)(2,1)S(1)}, u32[]{:S(2)}, u32[]{:S(2)}) collective-permute-start(bf16[2,12,72,256]{3,2,1,0:T(8,128)(2,1)S(1)} %bitcast.113), channel_id=1, source_target_pairs={{0,1},{1,2},{2,3},{4,5},{5,6},{6,7},{8,9},{9,10},{10,11},{12,13},{... | collective-permute-start | bytes 2654216 | tf_op jit(solution)/shard_map/ppermute | solution.py:19
  45.5 11.2 %collective-permute-start.4 = (bf16[2,12,72,256]{3,2,1,0:T(8,128)(2,1)S(1)}, bf16[2,12,72,256]{3,2,1,0:T(8,128)(2,1)S(1)}, u32[]{:S(2)}, u32[]{:S(2)}) collective-permute-start(bf16[2,12,72,256]{3,2,1,0:T(8,128)(2,1)S(1)} %bitcast.114), channel_id=1, source_target_pairs={{1,0},{2,1},{3,2},{5,4},{6,5},{7,6},{9,8},{10,9},{11,10},{13,12},{... | collective-permute-start | bytes 2654216 | tf_op jit(solution)/shard_map/ppermute | solution.py:20
  54.7 4.1 %slice-start = ((s8[5308416]{0:T(1024)(128)(4,1)}), s8[4194304]{0:T(1024)(128)(4,1)S(1)}, s32[]{:S(2)}) async-start(s8[5308416]{0:T(1024)(128)(4,1)} %bitcast.144), calls=%async_computation | async-start | bytes 8388608
  55.0 3.9 %slice-start.1 = ((s8[5308416]{0:T(1024)(128)(4,1)}), s8[1114112]{0:T(1024)(128)(4,1)S(1)}, s32[]{:S(2)}) async-start(s8[5308416]{0:T(1024)(128)(4,1)} %bitcast.144), calls=%async_computation.1 | async-start | bytes 2228224
  55.0 21.4 %collective-permute-start.6 = (f32[2,2,2,2,48,768]{5,4,3,1,0,2:T(8,128)S(1)}, f32[2,2,2,2,48,768]{5,4,3,1,0,2:T(8,128)S(1)}, u32[]{:S(2)}, u32[]{:S(2)}) collective-permute-start(f32[2,2,2,2,48,768]{5,4,3,1,0,2:T(8,128)S(1)} %bitcast.137), channel_id=1, source_target_pairs={{0,1},{1,0},{2,3},{3,2},{4,5},{5,4},{6,7},{7,6},{8,9},{9,8},{10,11... | collective-permute-start | bytes 7077896 | tf_op jit(solution)/shard_map/ppermute | solution.py:37
  64.0 12.3 %collective-permute-start.7 = (f32[2,2,2,2,48,768]{5,4,3,2,0,1:T(8,128)S(1)}, f32[2,2,2,2,48,768]{5,4,3,2,0,1:T(8,128)S(1)}, u32[]{:S(2)}, u32[]{:S(2)}) collective-permute-start(f32[2,2,2,2,48,768]{5,4,3,2,0,1:T(8,128)S(1)} %bitcast.138), channel_id=1, source_target_pairs={{0,1},{1,0},{2,3},{3,2},{4,5},{5,4},{6,7},{7,6},{8,9},{9,8},{10,11... | collective-permute-start | bytes 7077896 | tf_op jit(solution)/shard_map/ppermute | solution.py:37
  75.6 4.6 %collective-permute-start.5 = (f32[2,2,2,2,48,768]{5,4,2,1,0,3:T(8,128)S(1)}, f32[2,2,2,2,48,768]{5,4,2,1,0,3:T(8,128)S(1)}, u32[]{:S(2)}, u32[]{:S(2)}) collective-permute-start(f32[2,2,2,2,48,768]{5,4,2,1,0,3:T(8,128)S(1)} %bitcast.139), channel_id=1, source_target_pairs={{0,1},{1,0},{2,3},{3,2},{4,5},{5,4},{6,7},{7,6},{8,9},{9,8},{10,11... | collective-permute-start | bytes 7077896 | tf_op jit(solution)/shard_map/ppermute | solution.py:37
  81.6 28.4 %collective-permute-start.10 = (f32[2,2,2,48,768]{4,3,2,1,0:T(8,128)S(1)}, f32[2,2,2,48,768]{4,3,2,1,0:T(8,128)S(1)}, u32[]{:S(2)}, u32[]{:S(2)}) collective-permute-start(f32[2,2,2,48,768]{4,3,2,1,0:T(8,128)S(1)} %dynamic-slice_bitcast_fusion), channel_id=1, source_target_pairs={{0,8},{4,12},{8,0},{12,4},{16,24},{20,28},{24,16},{28,20},{1,9},{5... | collective-permute-start | bytes 3538952 | tf_op jit(solution)/shard_map/ppermute | solution.py:37
  82.1 27.9 %collective-permute-start.8 = (f32[2,2,2,48,768]{4,3,2,1,0:T(8,128)S(1)}, f32[2,2,2,48,768]{4,3,2,1,0:T(8,128)S(1)}, u32[]{:S(2)}, u32[]{:S(2)}) collective-permute-start(f32[2,2,2,48,768]{4,3,2,1,0:T(8,128)S(1)} %dynamic-slice_bitcast_fusion.2), channel_id=1, source_target_pairs={{0,2},{1,3},{2,0},{3,1},{4,6},{5,7},{6,4},{7,5},{8,10},{9,11},{10,... | collective-permute-start | bytes 3538952 | tf_op jit(solution)/shard_map/ppermute | solution.py:37
  82.1 27.9 %collective-permute-start.9 = (f32[2,2,2,48,768]{4,3,2,1,0:T(8,128)S(1)}, f32[2,2,2,48,768]{4,3,2,1,0:T(8,128)S(1)}, u32[]{:S(2)}, u32[]{:S(2)}) collective-permute-start(f32[2,2,2,48,768]{4,3,2,1,0:T(8,128)S(1)} %dynamic-slice_bitcast_fusion.1), channel_id=1, source_target_pairs={{0,4},{4,0},{8,12},{12,8},{16,20},{20,16},{24,28},{28,24},{1,5},{5... | collective-permute-start | bytes 3538952 | tf_op jit(solution)/shard_map/ppermute | solution.py:37
  83.6 26.4 %collective-permute-start.11 = (f32[1281]{0:T(1024)S(1)}, f32[1281]{0:T(1024)S(1)}, u32[]{:S(2)}, u32[]{:S(2)}) collective-permute-start(f32[1281]{0:T(1024)S(1)} %pad_maximum_fusion.2), channel_id=1, source_target_pairs={{0,4},{4,0},{8,12},{12,8},{16,20},{20,16},{24,28},{28,24},{1,5},{5... | collective-permute-start | bytes 15380 | tf_op jit(solution)/shard_map/ppermute | solution.py:37
  110.7 15.7 %collective-permute-start.12 = (f32[2,2,48,768]{3,2,1,0:T(8,128)S(1)}, f32[2,2,48,768]{3,2,1,0:T(8,128)S(1)}, u32[]{:S(2)}, u32[]{:S(2)}) collective-permute-start(f32[2,2,48,768]{3,2,1,0:T(8,128)S(1)} %dynamic-slice_bitcast_fusion.5), channel_id=1, source_target_pairs={{0,4},{4,0},{8,12},{12,8},{16,20},{20,16},{24,28},{28,24},{1,5},{5... | collective-permute-start | bytes 1769480 | tf_op jit(solution)/shard_map/ppermute | solution.py:37
  112.3 14.1 %collective-permute-start.13 = (f32[2,2,48,768]{3,2,1,0:T(8,128)S(1)}, f32[2,2,48,768]{3,2,1,0:T(8,128)S(1)}, u32[]{:S(2)}, u32[]{:S(2)}) collective-permute-start(f32[2,2,48,768]{3,2,1,0:T(8,128)S(1)} %dynamic-slice_bitcast_fusion.4), channel_id=1, source_target_pairs={{0,8},{4,12},{8,0},{12,4},{16,24},{20,28},{24,16},{28,20},{1,9},{5... | collective-permute-start | bytes 1769480 | tf_op jit(solution)/shard_map/ppermute | solution.py:37
  113.8 13.7 %collective-permute-start.14 = (f32[2,2,48,768]{3,2,1,0:T(8,128)S(1)}, f32[2,2,48,768]{3,2,1,0:T(8,128)S(1)}, u32[]{:S(2)}, u32[]{:S(2)}) collective-permute-start(f32[2,2,48,768]{3,2,1,0:T(8,128)S(1)} %dynamic-slice_bitcast_fusion.3), channel_id=1, source_target_pairs={{0,2},{1,3},{2,0},{3,1},{4,6},{5,7},{6,4},{7,5},{8,10},{9,11},{10,... | collective-permute-start | bytes 1769480 | tf_op jit(solution)/shard_map/ppermute | solution.py:37
  115.6 10.8 %collective-permute-start.15 = (f32[1281]{0:T(1024)S(1)}, f32[1281]{0:T(1024)S(1)}, u32[]{:S(2)}, u32[]{:S(2)}) collective-permute-start(f32[1281]{0:T(1024)S(1)} %add.186), channel_id=1, source_target_pairs={{0,8},{4,12},{8,0},{12,4},{16,24},{20,28},{24,16},{28,20},{1,9},{5... | collective-permute-start | bytes 15380 | tf_op jit(solution)/shard_map/ppermute | solution.py:37
  127.9 14.4 %collective-permute-start.16 = (f32[2,48,768]{2,1,0:T(8,128)S(1)}, f32[2,48,768]{2,1,0:T(8,128)S(1)}, u32[]{:S(2)}, u32[]{:S(2)}) collective-permute-start(f32[2,48,768]{2,1,0:T(8,128)S(1)} %dynamic-slice_bitcast_fusion.8), channel_id=1, source_target_pairs={{0,8},{4,12},{8,0},{12,4},{16,24},{20,28},{24,16},{28,20},{1,9},{5... | collective-permute-start | bytes 884744 | tf_op jit(solution)/shard_map/ppermute | solution.py:37
  128.4 13.9 %collective-permute-start.17 = (f32[2,48,768]{2,1,0:T(8,128)S(1)}, f32[2,48,768]{2,1,0:T(8,128)S(1)}, u32[]{:S(2)}, u32[]{:S(2)}) collective-permute-start(f32[2,48,768]{2,1,0:T(8,128)S(1)} %dynamic-slice_bitcast_fusion.7), channel_id=1, source_target_pairs={{0,16},{4,20},{8,24},{12,28},{16,0},{20,4},{24,8},{28,12},{1,17},{... | collective-permute-start | bytes 884744 | tf_op jit(solution)/shard_map/ppermute | solution.py:37
  131.0 11.3 %collective-permute-start.18 = (f32[2,48,768]{2,1,0:T(8,128)S(1)}, f32[2,48,768]{2,1,0:T(8,128)S(1)}, u32[]{:S(2)}, u32[]{:S(2)}) collective-permute-start(f32[2,48,768]{2,1,0:T(8,128)S(1)} %dynamic-slice_bitcast_fusion.6), channel_id=1, source_target_pairs={{0,4},{4,0},{8,12},{12,8},{16,20},{20,16},{24,28},{28,24},{1,5},{5... | collective-permute-start | bytes 884744 | tf_op jit(solution)/shard_map/ppermute | solution.py:37
  131.5 10.7 %collective-permute-start.19 = (f32[1281]{0:T(1024)S(1)}, f32[1281]{0:T(1024)S(1)}, u32[]{:S(2)}, u32[]{:S(2)}) collective-permute-start(f32[1281]{0:T(1024)S(1)} %add.194), channel_id=1, source_target_pairs={{0,16},{4,20},{8,24},{12,28},{16,0},{20,4},{24,8},{28,12},{1,17},{... | collective-permute-start | bytes 15380 | tf_op jit(solution)/shard_map/ppermute | solution.py:37
  144.1 9.8 %collective-permute-start.22 = (f32[48,768]{1,0:T(8,128)S(1)}, f32[48,768]{1,0:T(8,128)S(1)}, u32[]{:S(2)}, u32[]{:S(2)}) collective-permute-start(f32[48,768]{1,0:T(8,128)S(1)} %dynamic-slice_bitcast_fusion.9), channel_id=1, source_target_pairs={{0,16},{4,20},{8,24},{12,28},{16,0},{20,4},{24,8},{28,12},{1,17},{... | collective-permute-start | bytes 442376 | tf_op jit(solution)/shard_map/ppermute | solution.py:37
  150.4 8.3 %copy-start.1 = (f32[3,256]{1,0:T(4,128)S(1)}, f32[3,256]{1,0:T(4,128)}, u32[]{:S(2)}) copy-start(f32[3,256]{1,0:T(4,128)} %param.13) | copy-start | bytes 9220
  150.4 5.2 %collective-permute-start.21 = (f32[48,768]{1,0:T(8,128)S(1)}, f32[48,768]{1,0:T(8,128)S(1)}, u32[]{:S(2)}, u32[]{:S(2)}) collective-permute-start(f32[48,768]{1,0:T(8,128)S(1)} %dynamic-slice_bitcast_fusion.10), channel_id=1, source_target_pairs={{0,2},{1,3},{2,0},{3,1},{4,6},{5,7},{6,4},{7,5},{8,10},{9,11},{10,... | collective-permute-start | bytes 442376 | tf_op jit(solution)/shard_map/ppermute | solution.py:37
  151.7 6.1 %collective-permute-start.20 = (f32[48,768]{1,0:T(8,128)S(1)}, f32[48,768]{1,0:T(8,128)S(1)}, u32[]{:S(2)}, u32[]{:S(2)}) collective-permute-start(f32[48,768]{1,0:T(8,128)S(1)} %dynamic-slice_bitcast_fusion.11), channel_id=1, source_target_pairs={{0,16},{4,20},{8,24},{12,28},{16,0},{20,4},{24,8},{28,12},{1,17},{... | collective-permute-start | bytes 442376 | tf_op jit(solution)/shard_map/ppermute | solution.py:37
where the time goes:
time: 160 us
  matrix products  40 us (25%)
  waiting for transfers between devices  39.7 us (25%)
  starting transfers between devices  34.2 us (21%)
  blocking collectives  17.7 us (11%)
  other arithmetic  15.6 us (10%)
  local copies, waits for them, and re-layouts  6.95 us (4%)
  between operations  5.59 us (3%)
    ppermute x21, waiting for transfers between devices, exchange(): return lax.ppermute(x, axis, pairs)  39.7 us
    ppermute x21, starting transfers between devices, exchange(): return lax.ppermute(x, axis, pairs)  31.6 us
    dot_general x3, matrix products, body(): lax.dot_general(flat_x, cols, (((0,), (0,)), ((), ())), preferred_element...  18 us
    dot_general x2, matrix products, body(): lax.dot_general(shifted.reshape(local_pix, taps, out_chans), conv_weight[...  17.2 us
    psum x1, blocking collectives, body(): tile_stats = lax.psum(slot[:, None] * local_stats[None, :], 'tile')  11.2 us
    psum x1, blocking collectives, body(): lax.psum((jnp.sum(preactivation_gradient, 0), jnp.sum(preactivation_gradi...  6.56 us
  transfers between devices with their start and end apart: 23, of which 10 were waited for; matrix products, arithmetic and copies ran while one was open for 32% of the time, Pallas kernels for 0%

commit v1 on v0

--- a/solution.py
+++ b/solution.py
@@ -85,7 +85,7 @@
         [local_sum, jnp.sum(local_offset * local_offset, 0), jnp.sum(weights_pix)[None]]
     )
     slot = (jnp.arange(tiles) == lax.axis_index("tile")).astype(jnp.float32)
-    tile_stats = lax.psum(slot[:, None] * local_stats[None, :], "tile")
+    tile_stats = jnp.sum(lax.all_gather(slot[:, None] * local_stats[None, :], "tile"), axis=0)
     tile_sums = tile_stats[:, :out_chans]
     column_sum = jnp.sum(tile_sums, 0)
     tile_means = tile_sums / local_pix - column_sum / per_replica_part

time: 160 us -> 156 us (0.975)
  blocking collectives: 17.7 us -> 12.8 us
    psum x1 -> x0, blocking collectives: 11.2 us -> none  [body(): tile_stats = lax.psum(slot[:, None] * local_stats[None, :], 'tile')]
    all_gather x0 -> x1, blocking collectives: none -> 5.2 us  [body(): lax.all_gather(slot[:, None] * local_stats[None, :], 'tile')]
  transfers between devices with their start and end apart: 23 -> 23, of which waited for: 10 -> 10; matrix products, arithmetic and copies ran while one was open for 32% -> 33% of each run, Pallas kernels for 0% -> 0%
where the time goes in v1:
time: 156 us; the launch traced here: 155 us
  matrix products  40 us (26%)
  waiting for transfers between devices  39.7 us (25%)
  starting transfers between devices  34.4 us (22%)
  other arithmetic  15.6 us (10%)
  blocking collectives  12.8 us (8%)
  local copies, waits for them, and re-layouts  6.95 us (4%)
  between operations  5.59 us (4%)
    ppermute x21, waiting for transfers between devices, exchange(): return lax.ppermute(x, axis, pairs)  39.7 us
    ppermute x21, starting transfers between devices, exchange(): return lax.ppermute(x, axis, pairs)  31.8 us
    dot_general x3, matrix products, body(): lax.dot_general(flat_x, cols, (((0,), (0,)), ((), ())), preferred_element...  18 us
    dot_general x2, matrix products, body(): lax.dot_general(shifted.reshape(local_pix, taps, out_chans), conv_weight[...  17.1 us
    psum x1, blocking collectives, body(): lax.psum((jnp.sum(preactivation_gradient, 0), jnp.sum(preactivation_gradi...  7.6 us
    all_gather x1, blocking collectives, body(): lax.all_gather(slot[:, None] * local_stats[None, :], 'tile')  5.2 us
  transfers between devices with their start and end apart: 23, of which 10 were waited for; matrix products, arithmetic and copies ran while one was open for 33% of the time, Pallas kernels for 0%

profile of v1, /device:TPU:10, one launch (start us, length us, event | category | flops | bytes accessed | tf_op | source)
XLA Modules:
  0.0 155.1 jit_solution(15301423694830217334)
XLA Ops:
  0.7 0.8 copy.49
  1.6 0.7 convert_element_type.31
  2.2 1.4 convert_reduce_fusion
  3.6 1.5 multiply_reduce_fusion.1
  5.1 0.7 select_reduce_fusion.1
  5.8 0.7 pad_maximum_fusion.3
  6.5 5.2 %all_gather.4 = f32[4,4,513]{2,1,0:T(4,128)S(1)} all-gather(f32[1,4,513]{2,1,0:T(4,128)S(1)} %broadcast_multiply_fusion), channel_id=1, replica_groups=mesh['rep'=8,'tile'=4] {'tile'}, dimensions={0}, use_global_device_ids=true | all-gather | bytes 41040 | tf_op jit(solution)/shard_map/all_gather | solution.py:88
  11.7 0.6 slice_reduce_fusion.1
  12.3 0.5 collective-permute-start
  12.9 0.7 fusion.44
  13.8 1.8 %fusion.47 = (f32[1728]{0:T(1024)S(1)}, f32[1728,3]{0,1:T(4,128)S(1)}) fusion(f32[3,256]{1,0:T(4,128)S(1)} %copy-done, f32[1728,256]{1,0:T(8,128)S(1)} %fusion.26, f32[256]{0:T(256)S(1)} %copy-done.4, f32[256]{0:T(256)S(1)} %copy-done.3), kind=kOutput, calls=%fused_computation.130 | convolution fusion | flops 17255808 | bytes 1802240 | tf_op jit(solution)/shard_map/dot_general | solution.py:102
  15.6 0.6 multiply_reduce_fusion.2
  16.2 2.2 %fusion.45 = (f32[256]{0:T(256)S(1)}, f32[256]{0:T(256)S(1)}, f32[1728,256]{1,0:T(8,128)S(1)}) fusion(f32[256]{0:T(256)S(1)} %get-tuple-element.131, f32[256]{0:T(256)S(1)} %broadcast_multiply_fusion.2, bf16[2,12,72,256]{3,2,1,0:T(8,128)(2,1)S(1)} %copy-done.2, f32[3,256]{1,0:T(4,128)S(1)} %copy-done, f32[1728,3]{0,1:T(4,128)S(1)} %get-tuple-element.133, ...), kind=kOutput, calls=%fused_computation.128 | convolution fusion | flops 20374336 | bytes 4474368 | tf_op jit(solution)/shard_map/dot_general | solution.py:110
  18.4 1.0 fusion.27
  19.4 7.6 %all-reduce.2 = (f32[1]{0:T(128)}, f32[768]{0:T(1024)S(1)}, f32[256]{0:T(256)S(1)}, f32[256]{0:T(256)S(1)}) all-reduce(f32[1]{0:T(128)} %bitcast.2, f32[768]{0:T(1024)S(1)} %reshape.169, f32[256]{0:T(256)S(1)} %get-tuple-element.105, f32[256]{0:T(256)S(1)} %get-tuple-element.104), channel_id=1, replica_groups=mesh['rep'=8,'tile'=4] {'tile'}, use_global_device_ids=true, to_apply=%region_16.17 | all-reduce | flops 1281 | bytes 10248 | tf_op jit(solution)/shard_map/psum | solution.py:112
  27.0 0.7 pad_maximum_fusion.2
  29.0 1.8 %collective-permute-start.1 = (f32[]{:T(128)}, f32[]{:T(128)}, u32[]{:S(2)}, u32[]{:S(2)}) collective-permute-start(f32[]{:T(128)} %add.173), channel_id=1, source_target_pairs={{0,8},{4,12},{8,0},{12,4},{16,24},{20,28},{24,16},{28,20},{1,9},{5... | collective-permute-start | bytes 20 | tf_op jit(solution)/shard_map/ppermute | solution.py:37
  30.8 1.9 %collective-permute-done.1 = f32[]{:T(128)} collective-permute-done((f32[]{:T(128)}, f32[]{:T(128)}, u32[]{:S(2)}, u32[]{:S(2)}) %collective-permute-start.1) | collective-permute-done | bytes 36 | tf_op jit(solution)/shard_map/ppermute | solution.py:37
  33.3 3.9 %collective-permute-start.2 = (f32[]{:T(128)}, f32[]{:T(128)}, u32[]{:S(2)}, u32[]{:S(2)}) collective-permute-start(f32[]{:T(128)} %add.174), channel_id=1, source_target_pairs={{0,16},{4,20},{8,24},{12,28},{16,0},{20,4},{24,8},{28,12},{1,17},{... | collective-permute-start | bytes 20 | tf_op jit(solution)/shard_map/ppermute | solution.py:37
  37.3 0.7 collective-permute-done.2
  38.6 0.6 multiply_convert_fusion
  39.2 1.3 collective-permute-start.3
  40.5 1.3 collective-permute-start.4
  41.8 0.8 pad_slice_fusion.1
  42.7 6.7 %fusion.14 = f32[1536,768]{1,0:T(8,128)S(1)} fusion(bf16[1728,1536]{1,0:T(8,128)(2,1)} %bitcast.142, bf16[1728,256]{1,0:T(8,128)(2,1)S(1)} %bitcast.133, bf16[1728,256]{1,0:T(8,128)(2,1)S(1)} %multiply_convert_fusion, bf16[1728,256]{1,0:T(8,128)(2,1)S(1)} %bitcast.135), kind=kOutput, calls=%fused_computation.20 | convolution fusion | flops 4084826112 | bytes 12681216 | tf_op jit(solution)/shard_map/dot_general | solution.py:167
  49.4 0.4 constant_dynamic-slice_fusion.1
  50.0 1.9 %collective-permute-start.6 = (f32[2,2,2,2,48,768]{5,4,3,1,0,2:T(8,128)S(1)}, f32[2,2,2,2,48,768]{5,4,3,1,0,2:T(8,128)S(1)}, u32[]{:S(2)}, u32[]{:S(2)}) collective-permute-start(f32[2,2,2,2,48,768]{5,4,3,1,0,2:T(8,128)S(1)} %bitcast.137), channel_id=1, source_target_pairs={{0,1},{1,0},{2,3},{3,2},{4,5},{5,4},{6,7},{7,6},{8,9},{9,8},{10,11... | collective-permute-start | bytes 7077896 | tf_op jit(solution)/shard_map/ppermute | solution.py:37
  51.9 1.9 %fusion.5 = bf16[2,36,96,256]{3,2,1,0:T(8,128)(2,1)S(1)} fusion(bf16[2,12,72,256]{3,2,1,0:T(8,128)(2,1)S(1)} %collective-permute-done.4, bf16[2,12,72,256]{3,2,1,0:T(8,128)(2,1)S(1)} %bitcast.116, bf16[2,12,72,256]{3,2,1,0:T(8,128)(2,1)S(1)} %collective-permute-done.3), kind=kLoop, calls=%fused_computation.10 | loop fusion | flops 21233664 | bytes 6193152 | tf_op jit(solution)/shard_map/concatenate | solution.py:21
  53.8 0.3 fusion.46
  54.1 4.5 %fusion.20 = f32[1536,768]{1,0:T(8,128)S(1)} fusion(bf16[1728,1536]{1,0:T(8,128)(2,1)S(1)} %bitcast.146, bf16[1728,256]{1,0:T(8,128)(2,1)S(1)} %bitcast.125, bf16[1728,256]{1,0:T(8,128)(2,1)S(1)} %bitcast.121, bf16[1728,256]{1,0:T(8,128)(2,1)S(1)} %bitcast.127), kind=kOutput, calls=%fused_computation.26 | convolution fusion | flops 4084826112 | bytes 12681216 | tf_op jit(solution)/shard_map/dot_general | solution.py:167
  58.7 0.4 constant_dynamic-slice_fusion
  59.3 4.2 %collective-permute-start.7 = (f32[2,2,2,2,48,768]{5,4,3,2,0,1:T(8,128)S(1)}, f32[2,2,2,2,48,768]{5,4,3,2,0,1:T(8,128)S(1)}, u32[]{:S(2)}, u32[]{:S(2)}) collective-permute-start(f32[2,2,2,2,48,768]{5,4,3,2,0,1:T(8,128)S(1)} %bitcast.138), channel_id=1, source_target_pairs={{0,1},{1,0},{2,3},{3,2},{4,5},{5,4},{6,7},{7,6},{8,9},{9,8},{10,11... | collective-permute-start | bytes 7077896 | tf_op jit(solution)/shard_map/ppermute | solution.py:37
  63.5 6.7 %fusion.8 = f32[1536,768]{1,0:T(8,128)S(1)} fusion(bf16[1728,1536]{1,0:T(8,128)(2,1)} %bitcast.143, bf16[1728,256]{1,0:T(8,128)(2,1)S(1)} %bitcast.129, bf16[1728,256]{1,0:T(8,128)(2,1)S(1)} %bitcast.123, bf16[1728,256]{1,0:T(8,128)(2,1)S(1)} %bitcast.131), kind=kOutput, calls=%fused_computation.14 | convolution fusion | flops 4084826112 | bytes 12681216 | tf_op jit(solution)/shard_map/dot_general | solution.py:167
  70.3 0.4 constant_dynamic-slice_fusion.5
  71.6 3.9 %collective-permute-done.5 = f32[2,2,2,2,48,768]{5,4,2,1,0,3:T(8,128)S(1)} collective-permute-done((f32[2,2,2,2,48,768]{5,4,2,1,0,3:T(8,128)S(1)}, f32[2,2,2,2,48,768]{5,4,2,1,0,3:T(8,128)S(1)}, u32[]{:S(2)}, u32[]{:S(2)}) %collective-permute-start.5) | collective-permute-done | bytes 2359328 | tf_op jit(solution)/shard_map/ppermute | solution.py:37
  76.3 0.5 bitcast_add_fusion.2
  76.9 0.4 collective-permute-start.10
  77.3 1.6 %collective-permute-start.9 = (f32[2,2,2,48,768]{4,3,2,1,0:T(8,128)S(1)}, f32[2,2,2,48,768]{4,3,2,1,0:T(8,128)S(1)}, u32[]{:S(2)}, u32[]{:S(2)}) collective-permute-start(f32[2,2,2,48,768]{4,3,2,1,0:T(8,128)S(1)} %dynamic-slice_bitcast_fusion.1), channel_id=1, source_target_pairs={{0,4},{4,0},{8,12},{12,8},{16,20},{20,16},{24,28},{28,24},{1,5},{5... | collective-permute-start | bytes 3538952 | tf_op jit(solution)/shard_map/ppermute | solution.py:37
  78.9 0.4 collective-permute-start.11
  79.3 8.6 %bitcast_convert_fusion.1 = bf16[1728,768]{1,0:T(8,128)(2,1)S(1)} fusion(bf16[1728,9,256]{2,0,1:T(8,128)(2,1)S(1)} %constant_dynamic-update-slice_fusion, bf16[9,1536,256]{2,1,0:T(8,128)(2,1)} %param.10), kind=kOutput, calls=%fused_computation.5 | convolution fusion | flops 6116622336 | bytes 14155776 | tf_op jit(solution)/shard_map/dot_general | solution.py:174
  87.9 17.4 %collective-permute-done.11 = f32[1281]{0:T(1024)S(1)} collective-permute-done((f32[1281]{0:T(1024)S(1)}, f32[1281]{0:T(1024)S(1)}, u32[]{:S(2)}, u32[]{:S(2)}) %collective-permute-start.11) | collective-permute-done | bytes 5156 | tf_op jit(solution)/shard_map/ppermute | solution.py:37
  105.3 0.3 bitcast_add_fusion.3
  106.0 1.6 %collective-permute-start.12 = (f32[2,2,48,768]{3,2,1,0:T(8,128)S(1)}, f32[2,2,48,768]{3,2,1,0:T(8,128)S(1)}, u32[]{:S(2)}, u32[]{:S(2)}) collective-permute-start(f32[2,2,48,768]{3,2,1,0:T(8,128)S(1)} %dynamic-slice_bitcast_fusion.5), channel_id=1, source_target_pairs={{0,4},{4,0},{8,12},{12,8},{16,20},{20,16},{24,28},{28,24},{1,5},{5... | collective-permute-start | bytes 1769480 | tf_op jit(solution)/shard_map/ppermute | solution.py:37
  107.6 1.6 %collective-permute-start.13 = (f32[2,2,48,768]{3,2,1,0:T(8,128)S(1)}, f32[2,2,48,768]{3,2,1,0:T(8,128)S(1)}, u32[]{:S(2)}, u32[]{:S(2)}) collective-permute-start(f32[2,2,48,768]{3,2,1,0:T(8,128)S(1)} %dynamic-slice_bitcast_fusion.4), channel_id=1, source_target_pairs={{0,8},{4,12},{8,0},{12,4},{16,24},{20,28},{24,16},{28,20},{1,9},{5... | collective-permute-start | bytes 1769480 | tf_op jit(solution)/shard_map/ppermute | solution.py:37
  109.1 1.7 %collective-permute-start.14 = (f32[2,2,48,768]{3,2,1,0:T(8,128)S(1)}, f32[2,2,48,768]{3,2,1,0:T(8,128)S(1)}, u32[]{:S(2)}, u32[]{:S(2)}) collective-permute-start(f32[2,2,48,768]{3,2,1,0:T(8,128)S(1)} %dynamic-slice_bitcast_fusion.3), channel_id=1, source_target_pairs={{0,2},{1,3},{2,0},{3,1},{4,6},{5,7},{6,4},{7,5},{8,10},{9,11},{10,... | collective-permute-start | bytes 1769480 | tf_op jit(solution)/shard_map/ppermute | solution.py:37
  110.9 0.4 collective-permute-start.15
  111.3 8.6 %bitcast_convert_fusion = bf16[1728,768]{1,0:T(8,128)(2,1)S(1)} fusion(bf16[1728,9,256]{2,0,1:T(8,128)(2,1)S(1)} %constant_dynamic-update-slice_fusion, bf16[9,1536,256]{2,1,0:T(8,128)(2,1)} %param.10), kind=kOutput, calls=%fused_computation.4 | convolution fusion | flops 6116622336 | bytes 14155776 | tf_op jit(solution)/shard_map/dot_general | solution.py:174
  119.9 1.8 %collective-permute-done.15 = f32[1281]{0:T(1024)S(1)} collective-permute-done((f32[1281]{0:T(1024)S(1)}, f32[1281]{0:T(1024)S(1)}, u32[]{:S(2)}, u32[]{:S(2)}) %collective-permute-start.15) | collective-permute-done | bytes 5156 | tf_op jit(solution)/shard_map/ppermute | solution.py:37
  121.7 1.1 collective-permute-done.14
  123.1 0.5 collective-permute-start.16
  123.7 2.6 %collective-permute-start.17 = (f32[2,48,768]{2,1,0:T(8,128)S(1)}, f32[2,48,768]{2,1,0:T(8,128)S(1)}, u32[]{:S(2)}, u32[]{:S(2)}) collective-permute-start(f32[2,48,768]{2,1,0:T(8,128)S(1)} %dynamic-slice_bitcast_fusion.7), channel_id=1, source_target_pairs={{0,16},{4,20},{8,24},{12,28},{16,0},{20,4},{24,8},{28,12},{1,17},{... | collective-permute-start | bytes 884744 | tf_op jit(solution)/shard_map/ppermute | solution.py:37
  126.3 0.5 collective-permute-start.18
  126.8 0.4 collective-permute-start.19
  127.2 2.8 %pad_maximum_fusion = bf16[1728,1536]{1,0:T(8,128)(2,1)} fusion(bf16[1728,768]{1,0:T(8,128)(2,1)S(1)} %bitcast_convert_fusion, bf16[1728,768]{1,0:T(8,128)(2,1)S(1)} %bitcast_convert_fusion.1), kind=kLoop, calls=%fused_computation.3 | loop fusion | flops 10616832 | bytes 10616832 | tf_op jit(solution)/shard_map/concatenate | solution.py:225
  130.0 7.5 %collective-permute-done.19 = f32[1281]{0:T(1024)S(1)} collective-permute-done((f32[1281]{0:T(1024)S(1)}, f32[1281]{0:T(1024)S(1)}, u32[]{:S(2)}, u32[]{:S(2)}) %collective-permute-start.19) | collective-permute-done | bytes 5156 | tf_op jit(solution)/shard_map/ppermute | solution.py:37
  137.6 0.5 slice.75
  138.7 0.6 div.75
  139.4 6.2 %collective-permute-start.22 = (f32[48,768]{1,0:T(8,128)S(1)}, f32[48,768]{1,0:T(8,128)S(1)}, u32[]{:S(2)}, u32[]{:S(2)}) collective-permute-start(f32[48,768]{1,0:T(8,128)S(1)} %dynamic-slice_bitcast_fusion.9), channel_id=1, source_target_pairs={{0,16},{4,20},{8,24},{12,28},{16,0},{20,4},{24,8},{28,12},{1,17},{... | collective-permute-start | bytes 442376 | tf_op jit(solution)/shard_map/ppermute | solution.py:37
  145.7 1.2 collective-permute-start.21
  147.0 0.6 slice_divide_fusion.1
  147.6 1.6 %collective-permute-done.22 = f32[48,768]{1,0:T(8,128)S(1)} collective-permute-done((f32[48,768]{1,0:T(8,128)S(1)}, f32[48,768]{1,0:T(8,128)S(1)}, u32[]{:S(2)}, u32[]{:S(2)}) %collective-permute-start.22) | collective-permute-done | bytes 147488 | tf_op jit(solution)/shard_map/ppermute | solution.py:37
  149.2 1.7 %collective-permute-done.21 = f32[48,768]{1,0:T(8,128)S(1)} collective-permute-done((f32[48,768]{1,0:T(8,128)S(1)}, f32[48,768]{1,0:T(8,128)S(1)}, u32[]{:S(2)}, u32[]{:S(2)}) %collective-permute-start.21) | collective-permute-done | bytes 147488 | tf_op jit(solution)/shard_map/ppermute | solution.py:37
  150.9 2.1 %collective-permute-done.20 = f32[48,768]{1,0:T(8,128)S(1)} collective-permute-done((f32[48,768]{1,0:T(8,128)S(1)}, f32[48,768]{1,0:T(8,128)S(1)}, u32[]{:S(2)}, u32[]{:S(2)}) %collective-permute-start.20) | collective-permute-done | bytes 147488 | tf_op jit(solution)/shard_map/ppermute | solution.py:37
  153.2 0.8 copy.70
  (84 shorter events, 3.6 us)
Async XLA Ops:
  0.6 13.2 %copy-start = (f32[3,256]{1,0:T(4,128)S(1)}, f32[3,256]{1,0:T(4,128)}, u32[]{:S(2)}) copy-start(f32[3,256]{1,0:T(4,128)} %param.13) | copy-start | bytes 9220
  0.6 13.0 %copy-start.2 = (bf16[2,12,72,256]{3,2,1,0:T(8,128)(2,1)S(1)}, bf16[2,12,72,256]{3,2,1,0:T(8,128)(2,1)}, u32[]{:S(2)}) copy-start(bf16[2,12,72,256]{3,2,1,0:T(8,128)(2,1)} %param.9) | copy-start | bytes 2654212
  0.7 13.1 %copy-start.3 = (f32[256]{0:T(256)S(1)}, f32[256]{0:T(256)}, u32[]{:S(2)}) copy-start(f32[256]{0:T(256)} %param.11) | copy-start | bytes 3076
  0.7 13.1 %copy-start.4 = (f32[256]{0:T(256)S(1)}, f32[256]{0:T(256)}, u32[]{:S(2)}) copy-start(f32[256]{0:T(256)} %param.12) | copy-start | bytes 3076
  12.3 15.4 %collective-permute-start = (f32[]{:T(128)}, f32[]{:T(128)}, u32[]{:S(2)}, u32[]{:S(2)}) collective-permute-start(f32[]{:T(128)} %slice_reduce_fusion.1), channel_id=1, source_target_pairs={{0,4},{4,0},{8,12},{12,8},{16,20},{20,16},{24,28},{28,24},{1,5},{5... | collective-permute-start | bytes 20 | tf_op jit(solution)/shard_map/ppermute | solution.py:37
  29.0 3.7 %collective-permute-start.1 = (f32[]{:T(128)}, f32[]{:T(128)}, u32[]{:S(2)}, u32[]{:S(2)}) collective-permute-start(f32[]{:T(128)} %add.173), channel_id=1, source_target_pairs={{0,8},{4,12},{8,0},{12,4},{16,24},{20,28},{24,16},{28,20},{1,9},{5... | collective-permute-start | bytes 20 | tf_op jit(solution)/shard_map/ppermute | solution.py:37
  33.3 4.6 %collective-permute-start.2 = (f32[]{:T(128)}, f32[]{:T(128)}, u32[]{:S(2)}, u32[]{:S(2)}) collective-permute-start(f32[]{:T(128)} %add.174), channel_id=1, source_target_pairs={{0,16},{4,20},{8,24},{12,28},{16,0},{20,4},{24,8},{28,12},{1,17},{... | collective-permute-start | bytes 20 | tf_op jit(solution)/shard_map/ppermute | solution.py:37
  39.2 12.7 %collective-permute-start.3 = (bf16[2,12,72,256]{3,2,1,0:T(8,128)(2,1)S(1)}, bf16[2,12,72,256]{3,2,1,0:T(8,128)(2,1)S(1)}, u32[]{:S(2)}, u32[]{:S(2)}) collective-permute-start(bf16[2,12,72,256]{3,2,1,0:T(8,128)(2,1)S(1)} %bitcast.113), channel_id=1, source_target_pairs={{0,1},{1,2},{2,3},{4,5},{5,6},{6,7},{8,9},{9,10},{10,11},{12,13},{... | collective-permute-start | bytes 2654216 | tf_op jit(solution)/shard_map/ppermute | solution.py:19
  40.5 11.4 %collective-permute-start.4 = (bf16[2,12,72,256]{3,2,1,0:T(8,128)(2,1)S(1)}, bf16[2,12,72,256]{3,2,1,0:T(8,128)(2,1)S(1)}, u32[]{:S(2)}, u32[]{:S(2)}) collective-permute-start(bf16[2,12,72,256]{3,2,1,0:T(8,128)(2,1)S(1)} %bitcast.114), channel_id=1, source_target_pairs={{1,0},{2,1},{3,2},{5,4},{6,5},{7,6},{9,8},{10,9},{11,10},{13,12},{... | collective-permute-start | bytes 2654216 | tf_op jit(solution)/shard_map/ppermute | solution.py:20
  49.8 4.3 %slice-start = ((s8[5308416]{0:T(1024)(128)(4,1)}), s8[4194304]{0:T(1024)(128)(4,1)S(1)}, s32[]{:S(2)}) async-start(s8[5308416]{0:T(1024)(128)(4,1)} %bitcast.144), calls=%async_computation | async-start | bytes 8388608
  50.0 4.1 %slice-start.1 = ((s8[5308416]{0:T(1024)(128)(4,1)}), s8[1114112]{0:T(1024)(128)(4,1)S(1)}, s32[]{:S(2)}) async-start(s8[5308416]{0:T(1024)(128)(4,1)} %bitcast.144), calls=%async_computation.1 | async-start | bytes 2228224
  50.0 21.6 %collective-permute-start.6 = (f32[2,2,2,2,48,768]{5,4,3,1,0,2:T(8,128)S(1)}, f32[2,2,2,2,48,768]{5,4,3,1,0,2:T(8,128)S(1)}, u32[]{:S(2)}, u32[]{:S(2)}) collective-permute-start(f32[2,2,2,2,48,768]{5,4,3,1,0,2:T(8,128)S(1)} %bitcast.137), channel_id=1, source_target_pairs={{0,1},{1,0},{2,3},{3,2},{4,5},{5,4},{6,7},{7,6},{8,9},{9,8},{10,11... | collective-permute-start | bytes 7077896 | tf_op jit(solution)/shard_map/ppermute | solution.py:37
  59.3 12.3 %collective-permute-start.7 = (f32[2,2,2,2,48,768]{5,4,3,2,0,1:T(8,128)S(1)}, f32[2,2,2,2,48,768]{5,4,3,2,0,1:T(8,128)S(1)}, u32[]{:S(2)}, u32[]{:S(2)}) collective-permute-start(f32[2,2,2,2,48,768]{5,4,3,2,0,1:T(8,128)S(1)} %bitcast.138), channel_id=1, source_target_pairs={{0,1},{1,0},{2,3},{3,2},{4,5},{5,4},{6,7},{7,6},{8,9},{9,8},{10,11... | collective-permute-start | bytes 7077896 | tf_op jit(solution)/shard_map/ppermute | solution.py:37
  70.9 4.6 %collective-permute-start.5 = (f32[2,2,2,2,48,768]{5,4,2,1,0,3:T(8,128)S(1)}, f32[2,2,2,2,48,768]{5,4,2,1,0,3:T(8,128)S(1)}, u32[]{:S(2)}, u32[]{:S(2)}) collective-permute-start(f32[2,2,2,2,48,768]{5,4,2,1,0,3:T(8,128)S(1)} %bitcast.139), channel_id=1, source_target_pairs={{0,1},{1,0},{2,3},{3,2},{4,5},{5,4},{6,7},{7,6},{8,9},{9,8},{10,11... | collective-permute-start | bytes 7077896 | tf_op jit(solution)/shard_map/ppermute | solution.py:37
  76.9 28.4 %collective-permute-start.10 = (f32[2,2,2,48,768]{4,3,2,1,0:T(8,128)S(1)}, f32[2,2,2,48,768]{4,3,2,1,0:T(8,128)S(1)}, u32[]{:S(2)}, u32[]{:S(2)}) collective-permute-start(f32[2,2,2,48,768]{4,3,2,1,0:T(8,128)S(1)} %dynamic-slice_bitcast_fusion), channel_id=1, source_target_pairs={{0,8},{4,12},{8,0},{12,4},{16,24},{20,28},{24,16},{28,20},{1,9},{5... | collective-permute-start | bytes 3538952 | tf_op jit(solution)/shard_map/ppermute | solution.py:37
  77.3 28.0 %collective-permute-start.8 = (f32[2,2,2,48,768]{4,3,2,1,0:T(8,128)S(1)}, f32[2,2,2,48,768]{4,3,2,1,0:T(8,128)S(1)}, u32[]{:S(2)}, u32[]{:S(2)}) collective-permute-start(f32[2,2,2,48,768]{4,3,2,1,0:T(8,128)S(1)} %dynamic-slice_bitcast_fusion.2), channel_id=1, source_target_pairs={{0,2},{1,3},{2,0},{3,1},{4,6},{5,7},{6,4},{7,5},{8,10},{9,11},{10,... | collective-permute-start | bytes 3538952 | tf_op jit(solution)/shard_map/ppermute | solution.py:37
  77.3 28.0 %collective-permute-start.9 = (f32[2,2,2,48,768]{4,3,2,1,0:T(8,128)S(1)}, f32[2,2,2,48,768]{4,3,2,1,0:T(8,128)S(1)}, u32[]{:S(2)}, u32[]{:S(2)}) collective-permute-start(f32[2,2,2,48,768]{4,3,2,1,0:T(8,128)S(1)} %dynamic-slice_bitcast_fusion.1), channel_id=1, source_target_pairs={{0,4},{4,0},{8,12},{12,8},{16,20},{20,16},{24,28},{28,24},{1,5},{5... | collective-permute-start | bytes 3538952 | tf_op jit(solution)/shard_map/ppermute | solution.py:37
  78.9 26.4 %collective-permute-start.11 = (f32[1281]{0:T(1024)S(1)}, f32[1281]{0:T(1024)S(1)}, u32[]{:S(2)}, u32[]{:S(2)}) collective-permute-start(f32[1281]{0:T(1024)S(1)} %pad_maximum_fusion.2), channel_id=1, source_target_pairs={{0,4},{4,0},{8,12},{12,8},{16,20},{20,16},{24,28},{28,24},{1,5},{5... | collective-permute-start | bytes 15380 | tf_op jit(solution)/shard_map/ppermute | solution.py:37
  106.0 15.7 %collective-permute-start.12 = (f32[2,2,48,768]{3,2,1,0:T(8,128)S(1)}, f32[2,2,48,768]{3,2,1,0:T(8,128)S(1)}, u32[]{:S(2)}, u32[]{:S(2)}) collective-permute-start(f32[2,2,48,768]{3,2,1,0:T(8,128)S(1)} %dynamic-slice_bitcast_fusion.5), channel_id=1, source_target_pairs={{0,4},{4,0},{8,12},{12,8},{16,20},{20,16},{24,28},{28,24},{1,5},{5... | collective-permute-start | bytes 1769480 | tf_op jit(solution)/shard_map/ppermute | solution.py:37
  107.6 14.1 %collective-permute-start.13 = (f32[2,2,48,768]{3,2,1,0:T(8,128)S(1)}, f32[2,2,48,768]{3,2,1,0:T(8,128)S(1)}, u32[]{:S(2)}, u32[]{:S(2)}) collective-permute-start(f32[2,2,48,768]{3,2,1,0:T(8,128)S(1)} %dynamic-slice_bitcast_fusion.4), channel_id=1, source_target_pairs={{0,8},{4,12},{8,0},{12,4},{16,24},{20,28},{24,16},{28,20},{1,9},{5... | collective-permute-start | bytes 1769480 | tf_op jit(solution)/shard_map/ppermute | solution.py:37
  109.1 13.7 %collective-permute-start.14 = (f32[2,2,48,768]{3,2,1,0:T(8,128)S(1)}, f32[2,2,48,768]{3,2,1,0:T(8,128)S(1)}, u32[]{:S(2)}, u32[]{:S(2)}) collective-permute-start(f32[2,2,48,768]{3,2,1,0:T(8,128)S(1)} %dynamic-slice_bitcast_fusion.3), channel_id=1, source_target_pairs={{0,2},{1,3},{2,0},{3,1},{4,6},{5,7},{6,4},{7,5},{8,10},{9,11},{10,... | collective-permute-start | bytes 1769480 | tf_op jit(solution)/shard_map/ppermute | solution.py:37
  110.9 10.8 %collective-permute-start.15 = (f32[1281]{0:T(1024)S(1)}, f32[1281]{0:T(1024)S(1)}, u32[]{:S(2)}, u32[]{:S(2)}) collective-permute-start(f32[1281]{0:T(1024)S(1)} %add.184), channel_id=1, source_target_pairs={{0,8},{4,12},{8,0},{12,4},{16,24},{20,28},{24,16},{28,20},{1,9},{5... | collective-permute-start | bytes 15380 | tf_op jit(solution)/shard_map/ppermute | solution.py:37
  123.1 14.4 %collective-permute-start.16 = (f32[2,48,768]{2,1,0:T(8,128)S(1)}, f32[2,48,768]{2,1,0:T(8,128)S(1)}, u32[]{:S(2)}, u32[]{:S(2)}) collective-permute-start(f32[2,48,768]{2,1,0:T(8,128)S(1)} %dynamic-slice_bitcast_fusion.8), channel_id=1, source_target_pairs={{0,8},{4,12},{8,0},{12,4},{16,24},{20,28},{24,16},{28,20},{1,9},{5... | collective-permute-start | bytes 884744 | tf_op jit(solution)/shard_map/ppermute | solution.py:37
  123.7 13.9 %collective-permute-start.17 = (f32[2,48,768]{2,1,0:T(8,128)S(1)}, f32[2,48,768]{2,1,0:T(8,128)S(1)}, u32[]{:S(2)}, u32[]{:S(2)}) collective-permute-start(f32[2,48,768]{2,1,0:T(8,128)S(1)} %dynamic-slice_bitcast_fusion.7), channel_id=1, source_target_pairs={{0,16},{4,20},{8,24},{12,28},{16,0},{20,4},{24,8},{28,12},{1,17},{... | collective-permute-start | bytes 884744 | tf_op jit(solution)/shard_map/ppermute | solution.py:37
  126.3 11.3 %collective-permute-start.18 = (f32[2,48,768]{2,1,0:T(8,128)S(1)}, f32[2,48,768]{2,1,0:T(8,128)S(1)}, u32[]{:S(2)}, u32[]{:S(2)}) collective-permute-start(f32[2,48,768]{2,1,0:T(8,128)S(1)} %dynamic-slice_bitcast_fusion.6), channel_id=1, source_target_pairs={{0,4},{4,0},{8,12},{12,8},{16,20},{20,16},{24,28},{28,24},{1,5},{5... | collective-permute-start | bytes 884744 | tf_op jit(solution)/shard_map/ppermute | solution.py:37
  126.8 10.7 %collective-permute-start.19 = (f32[1281]{0:T(1024)S(1)}, f32[1281]{0:T(1024)S(1)}, u32[]{:S(2)}, u32[]{:S(2)}) collective-permute-start(f32[1281]{0:T(1024)S(1)} %add.192), channel_id=1, source_target_pairs={{0,16},{4,20},{8,24},{12,28},{16,0},{20,4},{24,8},{28,12},{1,17},{... | collective-permute-start | bytes 15380 | tf_op jit(solution)/shard_map/ppermute | solution.py:37
  139.4 9.8 %collective-permute-start.22 = (f32[48,768]{1,0:T(8,128)S(1)}, f32[48,768]{1,0:T(8,128)S(1)}, u32[]{:S(2)}, u32[]{:S(2)}) collective-permute-start(f32[48,768]{1,0:T(8,128)S(1)} %dynamic-slice_bitcast_fusion.9), channel_id=1, source_target_pairs={{0,16},{4,20},{8,24},{12,28},{16,0},{20,4},{24,8},{28,12},{1,17},{... | collective-permute-start | bytes 442376 | tf_op jit(solution)/shard_map/ppermute | solution.py:37
  145.6 8.3 %copy-start.1 = (f32[3,256]{1,0:T(4,128)S(1)}, f32[3,256]{1,0:T(4,128)}, u32[]{:S(2)}) copy-start(f32[3,256]{1,0:T(4,128)} %param.13) | copy-start | bytes 9220
  145.7 5.2 %collective-permute-start.21 = (f32[48,768]{1,0:T(8,128)S(1)}, f32[48,768]{1,0:T(8,128)S(1)}, u32[]{:S(2)}, u32[]{:S(2)}) collective-permute-start(f32[48,768]{1,0:T(8,128)S(1)} %dynamic-slice_bitcast_fusion.10), channel_id=1, source_target_pairs={{0,2},{1,3},{2,0},{3,1},{4,6},{5,7},{6,4},{7,5},{8,10},{9,11},{10,... | collective-permute-start | bytes 442376 | tf_op jit(solution)/shard_map/ppermute | solution.py:37
  146.9 6.1 %collective-permute-start.20 = (f32[48,768]{1,0:T(8,128)S(1)}, f32[48,768]{1,0:T(8,128)S(1)}, u32[]{:S(2)}, u32[]{:S(2)}) collective-permute-start(f32[48,768]{1,0:T(8,128)S(1)} %dynamic-slice_bitcast_fusion.11), channel_id=1, source_target_pairs={{0,16},{4,20},{8,24},{12,28},{16,0},{20,4},{24,8},{28,12},{1,17},{... | collective-permute-start | bytes 442376 | tf_op jit(solution)/shard_map/ppermute | solution.py:37
